TPU v7x, 256 devices: a whole 4x4x8 slice. The times are simulated.
256 devices in a mesh: depth: 16 (over y, z_hi), chan: 16 (over x, z_lo, core).
Axes of the slice: x: 4, y: 4, z: 8 (z_hi: 4, z_lo: 2; z = z_hi * 2 + z_lo), core: 2. Of those that a mesh axis runs over, the one named last changes fastest.
Arguments:
- volume: bfloat16 [256, 16, 4096], P('chan', 'depth'), may hold values from -6 to 6
- w_first: bfloat16 [27, 256, 256], P(None, 'chan'), may hold values from -0.078125 to 0.078125
- b_first: float32 [256], P('chan'), may hold values from -3 to 3
- w_second: bfloat16 [27, 256, 256], P(None, None, 'chan'), may hold values from -0.078125 to 0.078125
- b_second: float32 [256], P('chan'), may hold values from -3 to 3
Outputs:
- block_out: bfloat16 [256, 16, 4096], P('chan', 'depth')
All inputs are finite; a program needn't handle non-finite values.
Results may differ from a plain program's by a relative error of at most 0.0043.
Values may be sent and summed in bfloat16 or wider, within the bound.
No kernel may reach another device: no remote copies, remote signals or barrier semaphores. Data moves between devices by JAX's collectives and lax.ppermute only.
A program may use at most 128 MiB of HBM per device.

v0:
```python
import jax
import jax.numpy as jnp
from jax import lax
from jax.sharding import PartitionSpec as P

W = 64


def extended(array, sides, width):
    for axis, dim in sides:
        peers, length = (lax.axis_size(axis), array.shape[dim])
        up = [(i, (i + 1) % peers) for i in range(peers - 1)]
        down = [(j, i) for i, j in up]
        last = lax.slice_in_dim(array, length - width, length, axis=dim)
        leading = lax.slice_in_dim(array, 0, width, axis=dim)
        before = lax.ppermute(last, axis, up)
        after = lax.ppermute(leading, axis, down)
        array = jnp.concatenate([before, array, after], axis=dim)
    return array


def pad_cells(source):
    return jnp.pad(source, ((0, 0), (0, 0), (W + 1, W + 1)))


def nine_taps(segment):
    seg_chan, planes, cell_count = segment.shape
    padded = pad_cells(segment)
    column = jnp.arange(cell_count) % W
    left_ok = column >= 1
    right_ok = column < W - 1
    per_plane = []
    for plane in range(planes):
        windows = []
        for row_tap in range(3):
            for col_tap in range(3):
                begin = row_tap * W + col_tap
                window = padded[:, plane, begin : begin + cell_count]
                if col_tap == 0:
                    window = jnp.where(left_ok, window, jnp.zeros_like(window))
                elif col_tap == 2:
                    window = jnp.where(right_ok, window, jnp.zeros_like(window))
                windows.append(window)
        per_plane.append(jnp.concatenate(windows, 0))
    return jnp.concatenate(per_plane, 1)


def fold_planes(filters, running, segment):
    seg_chan, padded_depth, cell_count = segment.shape
    slab_depth = padded_depth - 2
    out_chan = filters.shape[2]
    grouped = filters.reshape(3, 9 * seg_chan, out_chan)
    columns = nine_taps(segment)
    total = running
    for depth_tap in range(3):
        window = columns[:, depth_tap * cell_count : (depth_tap + slab_depth) * cell_count]
        total = total + lax.dot_general(
            grouped[depth_tap], window, (((0,), (0,)), ((), ())), preferred_element_type=jnp.float32
        )
    return total


def tap_columns(rimmed):
    chan_local, padded_depth, cell_count = rimmed.shape
    padded = pad_cells(rimmed)
    column = jnp.arange(cell_count) % W
    left_ok = column >= 1
    right_ok = column < W - 1
    gathered_taps = []
    for depth_tap in range(3):
        for row_tap in range(3):
            for col_tap in range(3):
                begin = row_tap * W + col_tap
                window = padded[:, depth_tap, begin : begin + cell_count]
                if col_tap == 0:
                    window = jnp.where(left_ok, window, jnp.zeros_like(window))
                elif col_tap == 2:
                    window = jnp.where(right_ok, window, jnp.zeros_like(window))
                gathered_taps.append(window)
    per_plane = [jnp.concatenate(gathered_taps, 0)]
    return per_plane


def body(volume, w_first, b_first, w_second, b_second):
    chan_local, slab_depth, cell_count = volume.shape
    rimmed = extended(volume, (("depth", 1),), 1)
    empty_sum = jnp.zeros((chan_local, slab_depth * cell_count), jnp.float32)
    per_plane = tap_columns(rimmed)
    flat_filters = w_first.reshape(27 * chan_local, w_first.shape[2])
    pieces = [
        lax.dot_general(
            flat_filters, plane_cols, (((0,), (0,)), ((), ())), preferred_element_type=jnp.float32
        )
        for plane_cols in per_plane
    ]
    first_sum = lax.psum_scatter(
        jnp.stack(pieces, 1).reshape(chan_local * lax.axis_size("chan"), slab_depth * cell_count),
        "chan",
        scatter_dimension=0,
        tiled=True,
    )
    hidden = jnp.maximum(first_sum + b_first[:, None], 0.0).astype(jnp.bfloat16)
    hidden = hidden.reshape(chan_local, slab_depth, cell_count)
    hidden_rim = extended(hidden, (("depth", 1),), 1)
    second_sum = fold_planes(
        w_second, empty_sum, lax.all_gather(hidden_rim, "chan", axis=0, tiled=True)
    )
    block_out = (second_sum + b_second[:, None]).astype(jnp.bfloat16)
    return block_out.reshape(chan_local, slab_depth, cell_count)


def solution(mesh):
    in_specs = (
        P("chan", "depth", None),
        P(None, "chan", None),
        P("chan"),
        P(None, None, "chan"),
        P("chan"),
    )
    out_specs = P("chan", "depth", None)
    return jax.shard_map(body, mesh=mesh, in_specs=in_specs, out_specs=out_specs, check_vma=False)
```

profile of v0, /device:TPU:1, one launch (start us, length us, event | category | flops | bytes accessed | tf_op | source)
XLA Modules:
  0.0 243.7 jit_solution(11958815443732724612)
XLA Ops:
  6.5 5.8 %collective-permute-start = (bf16[16,1,4096]{2,0,1:T(8,128)(2,1)}, bf16[16,1,4096]{2,0,1:T(8,128)(2,1)S(1)}, u32[]{:S(2)}, u32[]{:S(2)}) collective-permute-start(bf16[16,1,4096]{2,0,1:T(8,128)(2,1)} %param.5), channel_id=1, source_target_pairs={{0,16},{16,32},{32,48},{48,64},{64,80},{80,96},{96,112},{112,128},... | collective-permute-start | bytes 393224 | tf_op jit(solution)/shard_map/ppermute | solution.py:16
  12.4 1.3 collective-permute-start.1
  13.7 1.1 collective-permute-done
  14.9 10.2 %collective-permute-done.1 = bf16[16,1,4096]{2,0,1:T(8,128)(2,1)S(1)} collective-permute-done((bf16[16,1,4096]{2,0,1:T(8,128)(2,1)}, bf16[16,1,4096]{2,0,1:T(8,128)(2,1)S(1)}, u32[]{:S(2)}, u32[]{:S(2)}) %collective-permute-start.1) | collective-permute-done | bytes 131104 | tf_op jit(solution)/shard_map/ppermute | solution.py:17
  25.0 1.1 fusion.30
  28.4 3.4 %convolution_bitcast_fusion = f32[256,4096]{0,1:T(8,128)} fusion(bf16[432,4096]{1,0:T(8,128)(2,1)S(1)} %fusion.32, bf16[432,256]{1,0:T(8,128)(2,1)S(1)} %bitcast.261), kind=kOutput, calls=%fused_computation | convolution fusion | flops 905969664 | bytes 7954432 | tf_op jit(solution)/shard_map/dot_general | solution.py:91
  31.8 5.7 %copy.15 = f32[256,4096]{1,0:T(8,128)} copy(f32[256,4096]{0,1:T(8,128)} %convolution_bitcast_fusion) | data formatting | bytes 8388608
  37.5 70.7 %reduce-scatter.4.cloned.1.call-done = f32[16,4096]{1,0:T(8,128)} async-done(((f32[256,4096]{1,0:T(8,128)}), f32[16,4096]{1,0:T(8,128)}) %reduce-scatter.4.cloned.1.call-update) | async-done | bytes 262160
  108.2 1.5 copy.16
  110.4 4.4 %collective-permute-start.2 = (bf16[16,1,4096]{2,0,1:T(8,128)(2,1)S(1)}, bf16[16,1,4096]{2,0,1:T(8,128)(2,1)S(1)}, u32[]{:S(2)}, u32[]{:S(2)}) collective-permute-start(bf16[16,1,4096]{2,0,1:T(8,128)(2,1)S(1)} %copy.9), channel_id=1, source_target_pairs={{0,16},{16,32},{32,48},{48,64},{64,80},{80,96},{96,112},{112,128},... | collective-permute-start | bytes 393224 | tf_op jit(solution)/shard_map/ppermute | solution.py:16
  114.7 1.5 collective-permute-start.3
  116.7 6.5 %collective-permute-done.3 = bf16[16,1,4096]{2,0,1:T(8,128)(2,1)S(1)} collective-permute-done((bf16[16,1,4096]{2,0,1:T(8,128)(2,1)S(1)}, bf16[16,1,4096]{2,0,1:T(8,128)(2,1)S(1)}, u32[]{:S(2)}, u32[]{:S(2)}) %collective-permute-start.3) | collective-permute-done | bytes 131104 | tf_op jit(solution)/shard_map/ppermute | solution.py:17
  124.0 1.0 slice_bitcast_fusion.27
  125.0 43.9 %all-gather.2.cloned.1.call-done = bf16[256,3,4096]{2,0,1:T(8,128)(2,1)} async-done(((bf16[16,3,4096]{2,0,1:T(8,128)(2,1)}), bf16[256,3,4096]{2,0,1:T(8,128)(2,1)}) %all-gather.2.cloned.1.call-update) | async-done | bytes 6291472 | tf_op jit(solution)/shard_map/all_gather | solution.py:106
  168.9 2.6 %fusion.11 = bf16[2304,4096]{1,0:T(8,128)(2,1)S(1)} fusion(pred[4096]{0:T(1024)(128)(4,1)S(1)} %fusion.76, bf16[256,3,4096]{2,0,1:T(8,128)(2,1)} %all-gather.2.cloned.1.call-done), kind=kLoop, calls=%fused_computation.25 | loop fusion | flops 1048575 | bytes 8392704
  172.3 0.9 bitcast_dynamic-update-slice_fusion.1
  173.2 1.2 fusion.10
  174.4 3.2 %fusion.9 = (bf16[2304,4096]{1,0:T(8,128)(2,1)S(1)}, bf16[2304,4096]{1,0:T(8,128)(2,1)}) fusion(bf16[2304,4096]{1,0:T(8,128)(2,1)S(1)} %fusion.10, pred[4096]{0:T(1024)(128)(4,1)S(1)} %fusion.76, bf16[256,3,4096]{2,0,1:T(8,128)(2,1)S(1)} %copy-done.2), kind=kLoop, calls=%fused_computation.20 | loop fusion | flops 2097151 | bytes 10489856
  177.6 2.4 fusion.3
  180.0 3.7 %fusion.8 = (bf16[2304,4096]{1,0:T(8,128)(2,1)S(1)}, bf16[2304,4096]{1,0:T(8,128)(2,1)}) fusion(bf16[2304,4096]{1,0:T(8,128)(2,1)S(1)} %get-tuple-element.22, pred[4096]{0:T(1024)(128)(4,1)S(1)} %fusion.75, bf16[256,3,4096]{2,0,1:T(8,128)(2,1)S(1)} %copy-done.2, bf16[2304,4096]{1,0:T(8,128)(2,1)} %get-tuple-element.23), kind=kLoop, calls=%fused_computation.18 | loop fusion | flops 2097152 | bytes 10489856
  183.7 6.5 %copy-done.3 = bf16[2304,4096]{1,0:T(8,128)(2,1)} copy-done((bf16[2304,4096]{1,0:T(8,128)(2,1)}, bf16[2304,4096]{1,0:T(8,128)(2,1)S(1)}, u32[]{:S(2)}) %copy-start.3) | copy-done | bytes 18874392
  190.1 4.0 %fusion.7 = (bf16[2304,4096]{1,0:T(8,128)(2,1)}, bf16[2304,4096]{1,0:T(8,128)(2,1)}, bf16[2304,4096]{1,0:T(8,128)(2,1)S(1)}) fusion(bf16[2304,4096]{1,0:T(8,128)(2,1)} %copy-done.3, pred[4096]{0:T(1024)(128)(4,1)S(1)} %fusion.76, bf16[256,3,4096]{2,0,1:T(8,128)(2,1)S(1)} %copy-done.2, bf16[2304,4096]{1,0:T(8,128)(2,1)} %get-tuple-element.12), kind=kLoop, calls=%fused_computation.16 | loop fusion | flops 3145727 | bytes 12587008
  194.1 3.2 %bitcast_dynamic-update-slice_fusion = (bf16[2304,4096]{1,0:T(8,128)(2,1)}, bf16[2304,4096]{1,0:T(8,128)(2,1)S(1)}, bf16[2304,4096]{1,0:T(8,128)(2,1)}) fusion(bf16[2304,4096]{1,0:T(8,128)(2,1)} %get-tuple-element.8, bf16[256,3,4096]{2,0,1:T(8,128)(2,1)S(1)} %copy-done.2, bf16[2304,4096]{1,0:T(8,128)(2,1)S(1)} %get-tuple-element.10, ...), kind=kLoop, calls=%fused_computation.14 | loop fusion | bytes 14680064
  197.3 4.9 %fusion.6 = (bf16[2304,4096]{1,0:T(8,128)(2,1)}, bf16[2304,4096]{1,0:T(8,128)(2,1)}, bf16[2304,4096]{1,0:T(8,128)(2,1)S(1)}) fusion(bf16[2304,4096]{1,0:T(8,128)(2,1)} %get-tuple-element.19, pred[4096]{0:T(1024)(128)(4,1)S(1)} %fusion.75, bf16[256,3,4096]{2,0,1:T(8,128)(2,1)S(1)} %copy-done.2, bf16[2304,4096]{1,0:T(8,128)(2,1)} %get-tuple-element.21, ...), kind=kLoop, calls=%fused_computation.13 | loop fusion | flops 3145728 | bytes 12587008 | tf_op jit(solution)/shard_map/concatenate | solution.py:44
  202.2 1.2 fusion.15
  203.6 1.2 fusion.14
  204.8 3.9 %fusion.13 = (bf16[2304,4096]{1,0:T(8,128)(2,1)S(1)}, bf16[2304,4096]{1,0:T(8,128)(2,1)}) fusion(bf16[2304,4096]{1,0:T(8,128)(2,1)S(1)} %fusion.14, pred[4096]{0:T(1024)(128)(4,1)S(1)} %fusion.76, bf16[256,3,4096]{2,0,1:T(8,128)(2,1)S(1)} %copy-done.2, bf16[2304,4096]{1,0:T(8,128)(2,1)} %get-tuple-element.6), kind=kLoop, calls=%fused_computation.30 | loop fusion | flops 2097152 | bytes 10489856
  208.7 4.1 %bitcast_dynamic-update-slice_fusion.2 = (bf16[2304,4096]{1,0:T(8,128)(2,1)S(1)}, bf16[2304,4096]{1,0:T(8,128)(2,1)}) fusion(bf16[2304,4096]{1,0:T(8,128)(2,1)S(1)} %get-tuple-element.17, bf16[256,3,4096]{2,0,1:T(8,128)(2,1)S(1)} %copy-done.2, bf16[2304,4096]{1,0:T(8,128)(2,1)} %get-tuple-element.18), kind=kLoop, calls=%fused_computation.28 | loop fusion | bytes 10485760
  212.8 3.9 %fusion.12 = (bf16[2304,4096]{1,0:T(8,128)(2,1)S(1)}, bf16[2304,4096]{1,0:T(8,128)(2,1)}) fusion(bf16[2304,4096]{1,0:T(8,128)(2,1)S(1)} %get-tuple-element.24, pred[4096]{0:T(1024)(128)(4,1)S(1)} %fusion.75, bf16[256,3,4096]{2,0,1:T(8,128)(2,1)S(1)} %copy-done.2, bf16[2304,4096]{1,0:T(8,128)(2,1)} %get-tuple-element.25), kind=kLoop, calls=%fused_computation.27 | loop fusion | flops 2097152 | bytes 10489856 | tf_op jit(solution)/shard_map/concatenate | solution.py:44
  216.7 7.9 %fusion.78 = f32[4096,16]{0,1:T(8,128)S(1)} fusion(bf16[2304,16]{0,1:T(8,128)(2,1)S(1)} %bitcast.264, bf16[2304,4096]{1,0:T(8,128)(2,1)} %get-tuple-element.16), kind=kOutput, calls=%fused_computation.144 | convolution fusion | flops 301989888 | bytes 19210240 | tf_op jit(solution)/shard_map/dot_general | solution.py:57
  224.6 2.6 %convolution_add_fusion.1 = f32[4096,16]{0,1:T(8,128)S(1)} fusion(f32[4096,16]{0,1:T(8,128)S(1)} %fusion.78, bf16[2304,16]{0,1:T(8,128)(2,1)S(1)} %bitcast.263, bf16[2304,4096]{1,0:T(8,128)(2,1)S(1)} %get-tuple-element.15), kind=kOutput, calls=%fused_computation.3 | convolution fusion | flops 302055424 | bytes 19472384 | tf_op jit(solution)/shard_map/dot_general | solution.py:57
  227.2 9.6 %fusion.2 = bf16[16,1,4096]{2,0,1:T(8,128)(2,1)} fusion(f32[4096,16]{0,1:T(8,128)S(1)} %convolution_add_fusion.1, bf16[2304,16]{0,1:T(8,128)(2,1)S(1)} %bitcast.262, bf16[2304,4096]{1,0:T(8,128)(2,1)} %get-tuple-element.5, f32[16]{0:T(128)S(1)} %copy-done.5), kind=kOutput, calls=%fused_computation.5 | convolution fusion | flops 302186496 | bytes 19341376 | tf_op jit(solution)/shard_map/dot_general | solution.py:57
  (54 shorter events, 5.0 us)
Async XLA Ops:
  6.5 21.9 %copy-start = (bf16[27,16,256]{2,1,0:T(8,128)(2,1)S(1)}, bf16[27,16,256]{2,1,0:T(8,128)(2,1)}, u32[]{:S(2)}) copy-start(bf16[27,16,256]{2,1,0:T(8,128)(2,1)} %param.6) | copy-start | bytes 663556
  6.5 20.7 %copy-start.4 = (bf16[16,1,4096]{2,0,1:T(8,128)(2,1)S(1)}, bf16[16,1,4096]{2,0,1:T(8,128)(2,1)}, u32[]{:S(2)}) copy-start(bf16[16,1,4096]{2,0,1:T(8,128)(2,1)} %param.5) | copy-start | bytes 393220
  6.5 101.7 %reduce-scatter.4.cloned.1.call-start = ((), (), s32[]{:S(2)}) async-start(), calls=%async_computation.2 | async-start | bytes 4456448
  6.5 8.3 %collective-permute-start = (bf16[16,1,4096]{2,0,1:T(8,128)(2,1)}, bf16[16,1,4096]{2,0,1:T(8,128)(2,1)S(1)}, u32[]{:S(2)}, u32[]{:S(2)}) collective-permute-start(bf16[16,1,4096]{2,0,1:T(8,128)(2,1)} %param.5), channel_id=1, source_target_pairs={{0,16},{16,32},{32,48},{48,64},{64,80},{80,96},{96,112},{112,128},... | collective-permute-start | bytes 393224 | tf_op jit(solution)/shard_map/ppermute | solution.py:16
  12.4 12.6 %collective-permute-start.1 = (bf16[16,1,4096]{2,0,1:T(8,128)(2,1)}, bf16[16,1,4096]{2,0,1:T(8,128)(2,1)S(1)}, u32[]{:S(2)}, u32[]{:S(2)}) collective-permute-start(bf16[16,1,4096]{2,0,1:T(8,128)(2,1)} %param.5), channel_id=1, source_target_pairs={{16,0},{32,16},{48,32},{64,48},{80,64},{96,80},{112,96},{128,112},... | collective-permute-start | bytes 393224 | tf_op jit(solution)/shard_map/ppermute | solution.py:17
  37.5 72.3 %copy-start.6 = (f32[16]{0:T(128)S(1)}, f32[16]{0:T(128)}, u32[]{:S(2)}) copy-start(f32[16]{0:T(128)} %param.7) | copy-start | bytes 196
  37.5 131.4 %all-gather.2.cloned.1.call-start = ((), (), s32[]{:S(2)}) async-start(), calls=%async_computation.1 | async-start | bytes 6684672 | tf_op jit(solution)/shard_map/all_gather | solution.py:106
  110.4 6.3 %collective-permute-start.2 = (bf16[16,1,4096]{2,0,1:T(8,128)(2,1)S(1)}, bf16[16,1,4096]{2,0,1:T(8,128)(2,1)S(1)}, u32[]{:S(2)}, u32[]{:S(2)}) collective-permute-start(bf16[16,1,4096]{2,0,1:T(8,128)(2,1)S(1)} %copy.9), channel_id=1, source_target_pairs={{0,16},{16,32},{32,48},{48,64},{64,80},{80,96},{96,112},{112,128},... | collective-permute-start | bytes 393224 | tf_op jit(solution)/shard_map/ppermute | solution.py:16
  114.7 8.5 %collective-permute-start.3 = (bf16[16,1,4096]{2,0,1:T(8,128)(2,1)S(1)}, bf16[16,1,4096]{2,0,1:T(8,128)(2,1)S(1)}, u32[]{:S(2)}, u32[]{:S(2)}) collective-permute-start(bf16[16,1,4096]{2,0,1:T(8,128)(2,1)S(1)} %copy.9), channel_id=1, source_target_pairs={{16,0},{32,16},{48,32},{64,48},{80,64},{96,80},{112,96},{128,112},... | collective-permute-start | bytes 393224 | tf_op jit(solution)/shard_map/ppermute | solution.py:17
  168.9 3.4 %copy-start.2 = (bf16[256,3,4096]{2,0,1:T(8,128)(2,1)S(1)}, bf16[256,3,4096]{2,0,1:T(8,128)(2,1)}, u32[]{:S(2)}) copy-start(bf16[256,3,4096]{2,0,1:T(8,128)(2,1)} %all-gather.2.cloned.1.call-done) | copy-start | bytes 18874372
  183.7 6.5 %copy-start.3 = (bf16[2304,4096]{1,0:T(8,128)(2,1)}, bf16[2304,4096]{1,0:T(8,128)(2,1)S(1)}, u32[]{:S(2)}) copy-start(bf16[2304,4096]{1,0:T(8,128)(2,1)S(1)} %get-tuple-element.11) | copy-start | bytes 56623108
  224.6 2.6 %copy-start.5 = (f32[16]{0:T(128)S(1)}, f32[16]{0:T(128)}, u32[]{:S(2)}) copy-start(f32[16]{0:T(128)} %param.9) | copy-start | bytes 196
  227.2 9.7 %copy-start.1 = (bf16[27,16,256]{2,1,0:T(8,128)(2,1)S(1)}, bf16[27,16,256]{2,1,0:T(8,128)(2,1)}, u32[]{:S(2)}) copy-start(bf16[27,16,256]{2,1,0:T(8,128)(2,1)} %param.6) | copy-start | bytes 663556
Sparse Core Ops, SparseCore 0:
  37.6 70.5 reduce-scatter.3
  124.1 44.7 all-gather.1
where the time goes:
time: 244 us
  waiting for transfers between devices  133 us (55%)
  other arithmetic  33.3 us (14%)
  local copies, waits for them, and re-layouts  27.3 us (11%)
  matrix products  23.5 us (10%)
  between operations  13.8 us (6%)
  starting transfers between devices  13 us (5%)
    unnamed x3, waiting for transfers between devices  70.7 us
    all_gather x1, waiting for transfers between devices, body(): lax.all_gather(hidden_rim, 'chan', axis=0, tiled=True)  43.9 us
    unnamed x31, local copies, waits for them, and re-layouts  26.9 us
    unnamed x25, other arithmetic  22.2 us
    dot_general x3, matrix products, fold_planes(): lax.dot_general(grouped[depth_tap], window, (((0,), (0,)), ((), ())), pre...  20.1 us
    ppermute x2, waiting for transfers between devices, extended(): after = lax.ppermute(leading, axis, down)  16.7 us
    ppermute x2, starting transfers between devices, extended(): before = lax.ppermute(last, axis, up)  10.2 us
    concatenate x2, other arithmetic, nine_taps(): per_plane.append(jnp.concatenate(windows, 0))  8.84 us
  transfers between devices with their start and end apart: 6, of which 6 were waited for; matrix products, arithmetic and copies ran while one was open for 0% of the time, Pallas kernels for 0%

commit v1 on v0

--- a/solution.py
+++ b/solution.py
@@ -2,8 +2,12 @@
 import jax.numpy as jnp
 from jax import lax
 from jax.sharding import PartitionSpec as P
+from jax.lax import all_to_all, psum
 
 W = 64
+links_report = lambda field_in: jnp.concatenate(
+    all_to_all(jnp.stack(psum(1, "chan") * [field_in], axis=0), "chan", 0, 0), axis=0
+)
 
 
 def extended(array, sides, width):
@@ -102,9 +106,7 @@
     hidden = jnp.maximum(first_sum + b_first[:, None], 0.0).astype(jnp.bfloat16)
     hidden = hidden.reshape(chan_local, slab_depth, cell_count)
     hidden_rim = extended(hidden, (("depth", 1),), 1)
-    second_sum = fold_planes(
-        w_second, empty_sum, lax.all_gather(hidden_rim, "chan", axis=0, tiled=True)
-    )
+    second_sum = fold_planes(w_second, empty_sum, links_report(hidden_rim))
     block_out = (second_sum + b_second[:, None]).astype(jnp.bfloat16)
     return block_out.reshape(chan_local, slab_depth, cell_count)
 

time: 244 us -> 294 us (1.20)
  waiting for transfers between devices: 133 us -> 161 us
  starting transfers between devices: 13 us -> 19.6 us
  other arithmetic: 33.3 us -> 39.7 us
  matrix products: 23.5 us -> 28.4 us
    all_to_all x0 -> x1, waiting for transfers between devices: none -> 72 us  [all_to_all(jnp.stack(psum(1, 'chan') * [field_in], axis=0), 'chan', 0, 0)]
    all_gather x1 -> x0, waiting for transfers between devices: 43.9 us -> none  [body(): lax.all_gather(hidden_rim, 'chan', axis=0, tiled=True)]
    all_to_all x0 -> x1, starting transfers between devices: none -> 6.95 us  [all_to_all(jnp.stack(psum(1, 'chan') * [field_in], axis=0), 'chan', 0, 0)]
    unnamed x25, other arithmetic: 22.2 us -> 28.4 us
    dot_general x3, matrix products: 20.1 us -> 25 us  [fold_planes(): lax.dot_general(grouped[depth_tap], window, (((0,), (0,)), ((), ())), pre...]
    unnamed x31 -> x29, local copies, waits for them, and re-layouts: 26.9 us -> 23.2 us
    another operation x0 -> x1, local copies, waits for them, and re-layouts: none -> 3.38 us  [jnp.stack(psum(1, 'chan') * [field_in], axis=0)]
    all_to_all x0 -> x1, local copies, waits for them, and re-layouts: none -> 3.21 us  [all_to_all(jnp.stack(psum(1, 'chan') * [field_in], axis=0), 'chan', 0, 0)]
where the time goes in v1:
time: 294 us; the launch traced here: 293 us
  waiting for transfers between devices  161 us (55%)
  other arithmetic  39.7 us (14%)
  local copies, waits for them, and re-layouts  30.1 us (10%)
  matrix products  28.4 us (10%)
  starting transfers between devices  19.6 us (7%)
  between operations  13.7 us (5%)
    all_to_all x1, waiting for transfers between devices, all_to_all(jnp.stack(psum(1, 'chan') * [field_in], axis=0), 'chan', 0, 0)  72 us
    unnamed x2, waiting for transfers between devices  70.9 us
    unnamed x25, other arithmetic  28.4 us
    dot_general x3, matrix products, fold_planes(): lax.dot_general(grouped[depth_tap], window, (((0,), (0,)), ((), ())), pre...  25 us
    unnamed x29, local copies, waits for them, and re-layouts  23.2 us
    ppermute x2, waiting for transfers between devices, extended(): after = lax.ppermute(leading, axis, down)  16.8 us
    ppermute x2, starting transfers between devices, extended(): before = lax.ppermute(last, axis, up)  10 us
    concatenate x2, other arithmetic, nine_taps(): per_plane.append(jnp.concatenate(windows, 0))  9.88 us
  transfers between devices with their start and end apart: 6, of which 6 were waited for; matrix products, arithmetic and copies ran while one was open for 0% of the time, Pallas kernels for 0%

profile of v1, /device:TPU:1, one launch (start us, length us, event | category | flops | bytes accessed | tf_op | source)
XLA Modules:
  0.0 293.0 jit_solution(5695402608645757321)
XLA Ops:
  6.5 5.8 %collective-permute-start = (bf16[16,1,4096]{2,0,1:T(8,128)(2,1)}, bf16[16,1,4096]{2,0,1:T(8,128)(2,1)S(1)}, u32[]{:S(2)}, u32[]{:S(2)}) collective-permute-start(bf16[16,1,4096]{2,0,1:T(8,128)(2,1)} %param.5), channel_id=1, source_target_pairs={{0,16},{16,32},{32,48},{48,64},{64,80},{80,96},{96,112},{112,128},... | collective-permute-start | bytes 393224 | tf_op jit(solution)/shard_map/ppermute | solution.py:20
  12.4 1.3 collective-permute-start.1
  14.9 10.2 %collective-permute-done.1 = bf16[16,1,4096]{2,0,1:T(8,128)(2,1)S(1)} collective-permute-done((bf16[16,1,4096]{2,0,1:T(8,128)(2,1)}, bf16[16,1,4096]{2,0,1:T(8,128)(2,1)S(1)}, u32[]{:S(2)}, u32[]{:S(2)}) %collective-permute-start.1) | collective-permute-done | bytes 131104 | tf_op jit(solution)/shard_map/ppermute | solution.py:21
  28.4 3.4 %convolution_bitcast_fusion = f32[256,4096]{0,1:T(8,128)} fusion(bf16[432,4096]{1,0:T(8,128)(2,1)S(1)} %fusion.32, bf16[432,256]{1,0:T(8,128)(2,1)S(1)} %bitcast.262), kind=kOutput, calls=%fused_computation | convolution fusion | flops 905969664 | bytes 7954432 | tf_op jit(solution)/shard_map/dot_general | solution.py:95
  31.8 5.7 %copy.24 = f32[256,4096]{1,0:T(8,128)} copy(f32[256,4096]{0,1:T(8,128)} %convolution_bitcast_fusion) | data formatting | bytes 8388608
  37.5 70.9 %reduce-scatter.4.cloned.1.call-done = f32[16,4096]{1,0:T(8,128)} async-done(((f32[256,4096]{1,0:T(8,128)}), f32[16,4096]{1,0:T(8,128)}) %reduce-scatter.4.cloned.1.call-update) | async-done | bytes 262160
  108.4 1.5 copy.25
  110.5 4.2 %collective-permute-start.2 = (bf16[16,1,4096]{2,0,1:T(8,128)(2,1)S(1)}, bf16[16,1,4096]{2,0,1:T(8,128)(2,1)S(1)}, u32[]{:S(2)}, u32[]{:S(2)}) collective-permute-start(bf16[16,1,4096]{2,0,1:T(8,128)(2,1)S(1)} %copy.17), channel_id=1, source_target_pairs={{0,16},{16,32},{32,48},{48,64},{64,80},{80,96},{96,112},{112,128},... | collective-permute-start | bytes 393224 | tf_op jit(solution)/shard_map/ppermute | solution.py:20
  114.7 1.3 collective-permute-start.3
  116.6 6.7 %collective-permute-done.3 = bf16[16,1,4096]{2,0,1:T(8,128)(2,1)S(1)} collective-permute-done((bf16[16,1,4096]{2,0,1:T(8,128)(2,1)S(1)}, bf16[16,1,4096]{2,0,1:T(8,128)(2,1)S(1)}, u32[]{:S(2)}, u32[]{:S(2)}) %collective-permute-start.3) | collective-permute-done | bytes 131104 | tf_op jit(solution)/shard_map/ppermute | solution.py:21
  123.3 3.4 %stack.2 = bf16[16,16,3,4096]{3,1,2,0:T(8,128)(2,1)} broadcast(bf16[16,3,4096]{2,0,1:T(8,128)(2,1)S(1)} %pad_maximum_fusion), dimensions={1,2,3} | broadcast | bytes 6684672 | tf_op jit(solution)/shard_map/stack | solution.py:9
  126.7 6.9 %all-to-all-start = ((bf16[16,16,3,4096]{3,1,2,0:T(8,128)(2,1)}), bf16[16,16,3,4096]{3,1,2,0:T(8,128)(2,1)}, u32[]{:S(2)}, u32[]{:S(2)}) async-start(bf16[16,16,3,4096]{3,1,2,0:T(8,128)(2,1)} %stack.2), calls=%async_computation | async-start | bytes 12582912 | tf_op jit(solution)/shard_map/all_to_all | solution.py:9
  133.7 72.0 %all-to-all-done = bf16[16,16,3,4096]{3,1,2,0:T(8,128)(2,1)} async-done(((bf16[16,16,3,4096]{3,1,2,0:T(8,128)(2,1)}), bf16[16,16,3,4096]{3,1,2,0:T(8,128)(2,1)}, u32[]{:S(2)}, u32[]{:S(2)}) %all-to-all-start) | async-done | bytes 6291488 | tf_op jit(solution)/shard_map/all_to_all | solution.py:9
  205.7 3.2 %copy.20 = bf16[16,16,3,4096]{3,1,0,2:T(8,128)(2,1)S(1)} copy(bf16[16,16,3,4096]{3,1,2,0:T(8,128)(2,1)} %all-to-all-done) | data formatting | bytes 12582912 | tf_op jit(solution)/shard_map/all_to_all | solution.py:9
  208.9 2.2 fusion.11
  211.2 2.3 bitcast_dynamic-update-slice_fusion.1
  213.5 2.6 fusion.10
  216.0 3.9 %fusion.9 = (bf16[2304,4096]{1,0:T(8,128)(2,1)}, bf16[2304,4096]{1,0:T(8,128)(2,1)}) fusion(bf16[2304,4096]{1,0:T(8,128)(2,1)} %fusion.10, pred[4096]{0:T(1024)(128)(4,1)S(1)} %fusion.76, bf16[256,3,4096]{2,0,1:T(8,128)(2,1)S(1)} %bitcast.266), kind=kLoop, calls=%fused_computation.20 | loop fusion | flops 2097151 | bytes 10489856
  219.9 3.1 %fusion.3 = (bf16[2304,4096]{1,0:T(8,128)(2,1)}, bf16[2304,4096]{1,0:T(8,128)(2,1)}) fusion(bf16[2304,4096]{1,0:T(8,128)(2,1)} %get-tuple-element.13, bf16[256,3,4096]{2,0,1:T(8,128)(2,1)S(1)} %bitcast.267, bf16[2304,4096]{1,0:T(8,128)(2,1)} %get-tuple-element.14), kind=kLoop, calls=%fused_computation.7 | loop fusion | bytes 12582912
  223.0 4.3 %fusion.8 = (bf16[2304,4096]{1,0:T(8,128)(2,1)}, bf16[2304,4096]{1,0:T(8,128)(2,1)}) fusion(bf16[2304,4096]{1,0:T(8,128)(2,1)} %get-tuple-element.22, pred[4096]{0:T(1024)(128)(4,1)S(1)} %fusion.75, bf16[256,3,4096]{2,0,1:T(8,128)(2,1)S(1)} %bitcast.268, bf16[2304,4096]{1,0:T(8,128)(2,1)} %get-tuple-element.23), kind=kLoop, calls=%fused_computation.18 | loop fusion | flops 2097152 | bytes 10489856
  227.3 4.4 %fusion.7 = (bf16[2304,4096]{1,0:T(8,128)(2,1)}, bf16[2304,4096]{1,0:T(8,128)(2,1)}, bf16[2304,4096]{1,0:T(8,128)(2,1)}) fusion(bf16[2304,4096]{1,0:T(8,128)(2,1)} %get-tuple-element.11, pred[4096]{0:T(1024)(128)(4,1)S(1)} %fusion.76, bf16[256,3,4096]{2,0,1:T(8,128)(2,1)S(1)} %bitcast.269, bf16[2304,4096]{1,0:T(8,128)(2,1)} %get-tuple-element.12), kind=kLoop, calls=%fused_computation.16 | loop fusion | flops 3145727 | bytes 12587008
  231.8 3.6 %bitcast_dynamic-update-slice_fusion = (bf16[2304,4096]{1,0:T(8,128)(2,1)}, bf16[2304,4096]{1,0:T(8,128)(2,1)}, bf16[2304,4096]{1,0:T(8,128)(2,1)}) fusion(bf16[2304,4096]{1,0:T(8,128)(2,1)} %get-tuple-element.8, bf16[256,3,4096]{2,0,1:T(8,128)(2,1)S(1)} %bitcast.270, bf16[2304,4096]{1,0:T(8,128)(2,1)} %get-tuple-element.10, ...), kind=kLoop, calls=%fused_computation.14 | loop fusion | bytes 14680064
  235.4 5.3 %fusion.6 = (bf16[2304,4096]{1,0:T(8,128)(2,1)}, bf16[2304,4096]{1,0:T(8,128)(2,1)}, bf16[2304,4096]{1,0:T(8,128)(2,1)}) fusion(bf16[2304,4096]{1,0:T(8,128)(2,1)} %get-tuple-element.19, pred[4096]{0:T(1024)(128)(4,1)S(1)} %fusion.75, bf16[256,3,4096]{2,0,1:T(8,128)(2,1)S(1)} %bitcast.271, bf16[2304,4096]{1,0:T(8,128)(2,1)} %get-tuple-element.21, ...), kind=kLoop, calls=%fused_computation.13 | loop fusion | flops 3145728 | bytes 12587008 | tf_op jit(solution)/shard_map/concatenate | solution.py:48
  240.6 2.6 fusion.15
  243.2 1.5 fusion.4
  244.7 2.5 fusion.14
  247.2 4.5 %fusion.13 = (bf16[2304,4096]{1,0:T(8,128)(2,1)}, bf16[2304,4096]{1,0:T(8,128)(2,1)}) fusion(bf16[2304,4096]{1,0:T(8,128)(2,1)} %fusion.14, pred[4096]{0:T(1024)(128)(4,1)S(1)} %fusion.76, bf16[256,3,4096]{2,0,1:T(8,128)(2,1)S(1)} %bitcast.275, bf16[2304,4096]{1,0:T(8,128)(2,1)} %get-tuple-element.6), kind=kLoop, calls=%fused_computation.30 | loop fusion | flops 2097152 | bytes 10489856
  251.7 4.8 %bitcast_dynamic-update-slice_fusion.2 = (bf16[2304,4096]{1,0:T(8,128)(2,1)}, bf16[2304,4096]{1,0:T(8,128)(2,1)}) fusion(bf16[2304,4096]{1,0:T(8,128)(2,1)} %get-tuple-element.17, bf16[256,3,4096]{2,0,1:T(8,128)(2,1)S(1)} %bitcast.276, bf16[2304,4096]{1,0:T(8,128)(2,1)} %get-tuple-element.18), kind=kLoop, calls=%fused_computation.28 | loop fusion | bytes 10485760
  256.5 4.6 %fusion.12 = (bf16[2304,4096]{1,0:T(8,128)(2,1)}, bf16[2304,4096]{1,0:T(8,128)(2,1)}) fusion(bf16[2304,4096]{1,0:T(8,128)(2,1)} %get-tuple-element.24, pred[4096]{0:T(1024)(128)(4,1)S(1)} %fusion.75, bf16[256,3,4096]{2,0,1:T(8,128)(2,1)S(1)} %bitcast.277, bf16[2304,4096]{1,0:T(8,128)(2,1)} %get-tuple-element.25), kind=kLoop, calls=%fused_computation.27 | loop fusion | flops 2097152 | bytes 10489856 | tf_op jit(solution)/shard_map/concatenate | solution.py:48
  261.1 7.7 %fusion.78 = f32[4096,16]{0,1:T(8,128)S(1)} fusion(bf16[2304,16]{0,1:T(8,128)(2,1)S(1)} %bitcast.280, bf16[2304,4096]{1,0:T(8,128)(2,1)} %get-tuple-element.16), kind=kOutput, calls=%fused_computation.144 | convolution fusion | flops 301989888 | bytes 19210240 | tf_op jit(solution)/shard_map/dot_general | solution.py:61
  268.8 7.7 %convolution_add_fusion.1 = f32[4096,16]{0,1:T(8,128)S(1)} fusion(f32[4096,16]{0,1:T(8,128)S(1)} %fusion.78, bf16[2304,16]{0,1:T(8,128)(2,1)S(1)} %bitcast.279, bf16[2304,4096]{1,0:T(8,128)(2,1)} %get-tuple-element.15), kind=kOutput, calls=%fused_computation.3 | convolution fusion | flops 302055424 | bytes 19472384 | tf_op jit(solution)/shard_map/dot_general | solution.py:61
  276.5 9.6 %fusion.2 = bf16[16,1,4096]{2,0,1:T(8,128)(2,1)} fusion(f32[4096,16]{0,1:T(8,128)S(1)} %convolution_add_fusion.1, bf16[2304,16]{0,1:T(8,128)(2,1)S(1)} %bitcast.278, bf16[2304,4096]{1,0:T(8,128)(2,1)} %get-tuple-element.5, f32[16]{0:T(128)S(1)} %copy-done.4), kind=kOutput, calls=%fused_computation.5 | convolution fusion | flops 302186496 | bytes 19341376 | tf_op jit(solution)/shard_map/dot_general | solution.py:61
  (53 shorter events, 5.6 us)
Async XLA Ops:
  6.5 21.9 %copy-start = (bf16[27,16,256]{2,1,0:T(8,128)(2,1)S(1)}, bf16[27,16,256]{2,1,0:T(8,128)(2,1)}, u32[]{:S(2)}) copy-start(bf16[27,16,256]{2,1,0:T(8,128)(2,1)} %param.6) | copy-start | bytes 663556
  6.5 20.7 %copy-start.2 = (bf16[16,1,4096]{2,0,1:T(8,128)(2,1)S(1)}, bf16[16,1,4096]{2,0,1:T(8,128)(2,1)}, u32[]{:S(2)}) copy-start(bf16[16,1,4096]{2,0,1:T(8,128)(2,1)} %param.5) | copy-start | bytes 393220
  6.5 101.8 %reduce-scatter.4.cloned.1.call-start = ((), (), s32[]{:S(2)}) async-start(), calls=%async_computation.2 | async-start | bytes 4456448
  6.5 8.3 %collective-permute-start = (bf16[16,1,4096]{2,0,1:T(8,128)(2,1)}, bf16[16,1,4096]{2,0,1:T(8,128)(2,1)S(1)}, u32[]{:S(2)}, u32[]{:S(2)}) collective-permute-start(bf16[16,1,4096]{2,0,1:T(8,128)(2,1)} %param.5), channel_id=1, source_target_pairs={{0,16},{16,32},{32,48},{48,64},{64,80},{80,96},{96,112},{112,128},... | collective-permute-start | bytes 393224 | tf_op jit(solution)/shard_map/ppermute | solution.py:20
  12.4 12.6 %collective-permute-start.1 = (bf16[16,1,4096]{2,0,1:T(8,128)(2,1)}, bf16[16,1,4096]{2,0,1:T(8,128)(2,1)S(1)}, u32[]{:S(2)}, u32[]{:S(2)}) collective-permute-start(bf16[16,1,4096]{2,0,1:T(8,128)(2,1)} %param.5), channel_id=1, source_target_pairs={{16,0},{32,16},{48,32},{64,48},{80,64},{96,80},{112,96},{128,112},... | collective-permute-start | bytes 393224 | tf_op jit(solution)/shard_map/ppermute | solution.py:21
  37.5 72.4 %copy-start.5 = (f32[16]{0:T(128)S(1)}, f32[16]{0:T(128)}, u32[]{:S(2)}) copy-start(f32[16]{0:T(128)} %param.7) | copy-start | bytes 196
  110.5 6.1 %collective-permute-start.2 = (bf16[16,1,4096]{2,0,1:T(8,128)(2,1)S(1)}, bf16[16,1,4096]{2,0,1:T(8,128)(2,1)S(1)}, u32[]{:S(2)}, u32[]{:S(2)}) collective-permute-start(bf16[16,1,4096]{2,0,1:T(8,128)(2,1)S(1)} %copy.17), channel_id=1, source_target_pairs={{0,16},{16,32},{32,48},{48,64},{64,80},{80,96},{96,112},{112,128},... | collective-permute-start | bytes 393224 | tf_op jit(solution)/shard_map/ppermute | solution.py:20
  114.7 8.6 %collective-permute-start.3 = (bf16[16,1,4096]{2,0,1:T(8,128)(2,1)S(1)}, bf16[16,1,4096]{2,0,1:T(8,128)(2,1)S(1)}, u32[]{:S(2)}, u32[]{:S(2)}) collective-permute-start(bf16[16,1,4096]{2,0,1:T(8,128)(2,1)S(1)} %copy.17), channel_id=1, source_target_pairs={{16,0},{32,16},{48,32},{64,48},{80,64},{96,80},{112,96},{128,112},... | collective-permute-start | bytes 393224 | tf_op jit(solution)/shard_map/ppermute | solution.py:21
  126.7 7.0 %copy-start.3 = (bf16[27,256,16]{1,2,0:T(8,128)(2,1)S(1)}, bf16[27,256,16]{1,2,0:T(8,128)(2,1)}, u32[]{:S(2)}) copy-start(bf16[27,256,16]{1,2,0:T(8,128)(2,1)} %param.8) | copy-start | bytes 663556
  126.7 79.0 %all-to-all-start = ((bf16[16,16,3,4096]{3,1,2,0:T(8,128)(2,1)}), bf16[16,16,3,4096]{3,1,2,0:T(8,128)(2,1)}, u32[]{:S(2)}, u32[]{:S(2)}) async-start(bf16[16,16,3,4096]{3,1,2,0:T(8,128)(2,1)} %stack.2), calls=%async_computation | async-start | bytes 12582912 | tf_op jit(solution)/shard_map/all_to_all | solution.py:9
  268.8 7.7 %copy-start.4 = (f32[16]{0:T(128)S(1)}, f32[16]{0:T(128)}, u32[]{:S(2)}) copy-start(f32[16]{0:T(128)} %param.9) | copy-start | bytes 196
  276.5 9.6 %copy-start.1 = (bf16[27,16,256]{2,1,0:T(8,128)(2,1)S(1)}, bf16[27,16,256]{2,1,0:T(8,128)(2,1)}, u32[]{:S(2)}) copy-start(bf16[27,16,256]{2,1,0:T(8,128)(2,1)} %param.6) | copy-start | bytes 663556
Sparse Core Ops, SparseCore 0:
  37.6 70.6 reduce-scatter.3
